TPU v7x, 32 devices: a whole 2x2x4 slice. The times are simulated.
32 devices in a mesh: gx: 8 (over z, core), gy: 4 (over y, x).
Axes of the slice: x: 2, y: 2, z: 4, core: 2. Of those that a mesh axis runs over, the one named last changes fastest.
Arguments:
- pressure: float32 [256, 128, 512], P('gx', 'gy'), may hold values from -6 to 6
- vel_x: float32 [256, 128, 512], P('gx', 'gy'), may hold values from -3 to 3
- vel_y: float32 [256, 128, 512], P('gx', 'gy'), may hold values from -3 to 3
- vel_z: float32 [256, 128, 512], P('gx', 'gy'), may hold values from -3 to 3
- void_frac: float32 [256, 128, 512], P('gx', 'gy'), may hold values from 1e-05 to 0.001
- waves: bfloat16 [24576, 2, 512], P(('gx', 'gy')), may hold values from -6 to 6
- bubble_dest: int32 [24576, 1], P(('gx', 'gy')), may hold values from 0 to 31; in each aligned block of 768 rows (0 to 767, 768 to 1535, ...) at most 48 rows name the same one
- bubble_column: int32 [24576], P(('gx', 'gy')), may hold values from 0 to 1023
- history: bfloat16 [128, 128, 512], P('gx', 'gy'), may hold values from -3 to 3
- delays: int32 [8, 8], replicated, may hold values from 0 to 15
Outputs:
- pressure_out: float32 [256, 128, 512], P('gx', 'gy')
- vel_x_out: float32 [256, 128, 512], P('gx', 'gy')
- vel_y_out: float32 [256, 128, 512], P('gx', 'gy')
- vel_z_out: float32 [256, 128, 512], P('gx', 'gy')
Inputs may be any that keep to these rules, and one draw needn't show every extreme that they name: `bubble_dest`: among the 768 bubbles listed on one device (an aligned block of rows), no tile is named more than 48 times.
All inputs are finite; a program needn't handle non-finite values.
Results may differ from a plain program's by a relative error of at most 0.00045.
Values may be sent and summed in bfloat16 or wider, within the bound.
No kernel may reach another device: no remote copies, remote signals or barrier semaphores. Data moves between devices by JAX's collectives and lax.ppermute only.
A program may use at most 128 MiB of HBM per device.

v0:
```python
import jax
import jax.numpy as jnp
from jax import lax
from jax.sharding import PartitionSpec as P

step_ratio = 0.4
gas_density = 0.001
gas_stiffness = 5.29e-05


def from_behind(block, axis, distance):
    devices = range(lax.axis_size(axis))
    route = [(i - distance, i) for i in devices if i - distance in devices]
    return lax.ppermute(block, axis, route)


def material(void_frac):
    liquid = 1.0 - void_frac
    buoyancy = 1.0 / (liquid + void_frac * gas_density)
    stiffness = 1.0 / (liquid + void_frac / gas_stiffness)
    return (buoyancy, stiffness)


def bubble_source(waves, bubble_dest, bubble_column, cells, ready):
    tiles_x = lax.axis_size("gx")
    tiles_y = lax.axis_size("gy")
    devices = tiles_x * tiles_y
    bubbles = waves.shape[0]
    steps = waves.shape[1]
    depth = waves.shape[2]
    capacity = 2 * bubbles // devices
    slots = devices * capacity
    me = lax.axis_index("gx") * tiles_y + lax.axis_index("gy")
    dest = bubble_dest[:, 0]
    owners = (dest[:, None] == jnp.arange(devices, dtype=jnp.int32)[None, :]).astype(jnp.int32)
    rank = jnp.sum(jnp.cumsum(owners, axis=0) * owners, axis=1) - 1
    slot_ids = dest * capacity + rank
    placed = slot_ids[None, :] == jnp.arange(slots, dtype=jnp.int32)[:, None]
    outgoing = jnp.dot(
        placed.astype(jnp.bfloat16),
        waves.reshape(bubbles, steps * depth),
        preferred_element_type=jnp.float32,
    ).astype(jnp.bfloat16)
    code = dest * cells + bubble_column
    all_code = lax.all_gather(code, ("gx", "gy"), axis=0, tiled=True).reshape(devices, bubbles)
    all_dest = all_code // cells
    all_col = all_code % cells
    mine = (all_dest == me).astype(jnp.int32)
    in_rank = jnp.cumsum(mine, axis=1) - 1
    in_rank = jnp.where(mine > 0, in_rank, -1)
    slot_of = jnp.arange(capacity, dtype=jnp.int32)
    match = in_rank[:, None, :] == slot_of[None, :, None]
    in_cols = jnp.max(jnp.where(match, all_col[:, None, :] + 1, 0), axis=2) - 1
    in_cols, outgoing, ready = lax.optimization_barrier((in_cols, outgoing, ready))
    incoming = lax.all_to_all(
        outgoing.reshape(devices, capacity, steps * depth),
        ("gx", "gy"),
        split_axis=0,
        concat_axis=0,
        tiled=True,
    )
    hits = (jnp.arange(cells, dtype=jnp.int32)[:, None] == in_cols.reshape(slots)[None, :]).astype(
        jnp.bfloat16
    )
    source = jnp.dot(
        hits, incoming.reshape(slots, steps * depth), preferred_element_type=jnp.float32
    )
    return (source, ready)


def incident_plane(history, delays, size_y, depth):
    tiles_x = lax.axis_size("gx")
    my_tile = lax.axis_index("gx")
    cycle = jnp.arange(tiles_x, dtype=jnp.int32)
    dist = jnp.abs(cycle - my_tile)
    dist = jnp.minimum(dist, tiles_x - dist)
    weight = 1.0 / (1.0 + 2.0 * dist.astype(jnp.float32) / tiles_x)
    wanted = lax.dynamic_index_in_dim(delays, my_tile, 1, keepdims=False)
    chosen = jnp.take(history, wanted, axis=0)
    rows = lax.all_to_all(chosen, "gx", split_axis=0, concat_axis=0, tiled=True)
    return jnp.sum(weight[:, None, None] * rows.astype(jnp.float32), axis=0)


def body(
    pressure, vel_x, vel_y, vel_z, void_frac, waves, bubble_dest, bubble_column, history, delays
):
    size_x, size_y, depth = pressure.shape
    steps = waves.shape[1]
    ix = lax.axis_index("gx")
    iy = lax.axis_index("gy")
    has_below_x = ix > 0
    has_below_y = iy > 0
    buoyancy, stiffness = material(void_frac)
    above_x = from_behind(pressure[0:1], "gx", -1)
    above_y = from_behind(pressure[:, 0:1], "gy", -1)
    below_x = from_behind(jnp.concatenate([pressure[-1:], vel_x[-1:], void_frac[-1:]], 0), "gx", 1)
    below_y = from_behind(
        jnp.concatenate([pressure[:, -1:], vel_y[:, -1:], void_frac[:, -1:]], 1), "gy", 1
    )
    incident = incident_plane(history, delays, size_y, depth)
    ready = (above_x, above_y, below_x, below_y, incident)
    source, ready = bubble_source(waves, bubble_dest, bubble_column, size_x * size_y, ready)
    above_x, above_y, below_x, below_y, incident = ready
    source = source.reshape(size_x, size_y, steps, depth)
    p_bx, vx_bx, void_bx = (below_x[0:1], below_x[1:2], below_x[2:3])
    p_by, vy_by, void_by = (below_y[:, 0:1], below_y[:, 1:2], below_y[:, 2:3])
    b_bx, _ = material(void_bx)
    b_by, _ = material(void_by)
    forcing = jnp.zeros_like(pressure).at[0].set(incident)
    z_edge = jnp.zeros((size_x, size_y, 1), jnp.float32)
    for step in range(steps):
        next_x = jnp.concatenate([pressure[1:], above_x], 0)
        next_y = jnp.concatenate([pressure[:, 1:], above_y], 1)
        next_z = jnp.concatenate([pressure[:, :, 1:], z_edge], 2)
        vel_x = vel_x - step_ratio * buoyancy * (next_x - pressure)
        vel_y = vel_y - step_ratio * buoyancy * (next_y - pressure)
        vel_z = vel_z - step_ratio * buoyancy * (next_z - pressure)
        vx_bx = vx_bx - step_ratio * b_bx * (pressure[0:1] - p_bx)
        vy_by = vy_by - step_ratio * b_by * (pressure[:, 0:1] - p_by)
        lower_x = jnp.where(has_below_x, vx_bx, 0.0)
        lower_y = jnp.where(has_below_y, vy_by, 0.0)
        prev_x = jnp.concatenate([lower_x, vel_x[:-1]], 0)
        prev_y = jnp.concatenate([lower_y, vel_y[:, :-1]], 1)
        prev_z = jnp.concatenate([z_edge, vel_z[:, :, :-1]], 2)
        divergence = vel_x - prev_x + (vel_y - prev_y) + (vel_z - prev_z)
        pressure = pressure + step_ratio * stiffness * (
            source[:, :, step, :] + forcing - divergence
        )
        if step + 1 < steps:
            above_x = from_behind(pressure[0:1], "gx", -1)
            above_y = from_behind(pressure[:, 0:1], "gy", -1)
            p_bx = from_behind(pressure[-1:], "gx", 1)
            p_by = from_behind(pressure[:, -1:], "gy", 1)
    return (pressure, vel_x, vel_y, vel_z)


def solution(mesh):
    in_specs = (
        P("gx", "gy", None),
        P("gx", "gy", None),
        P("gx", "gy", None),
        P("gx", "gy", None),
        P("gx", "gy", None),
        P(("gx", "gy"), None, None),
        P(("gx", "gy"), None),
        P(("gx", "gy")),
        P("gx", "gy", None),
        P(),
    )
    out_specs = (P("gx", "gy", None), P("gx", "gy", None), P("gx", "gy", None), P("gx", "gy", None))
    return jax.shard_map(body, mesh=mesh, in_specs=in_specs, out_specs=out_specs, check_vma=False)
```

profile of v0, /device:TPU:0, one launch (start us, length us, event | category | flops | bytes accessed | tf_op | source)
XLA Modules:
  0.0 215.8 jit_solution(4152463765882377466)
XLA Ops:
  0.7 1.4 fusion.50
  2.0 1.3 collective-permute-start.1
  3.3 0.9 fusion.51
  4.2 1.3 collective-permute-start
  7.3 3.2 %collective-permute-start.2 = (f32[3,32,512]{2,1,0:T(8,128)S(1)}, f32[3,32,512]{2,1,0:T(8,128)S(1)}, u32[]{:S(2)}, u32[]{:S(2)}) collective-permute-start(f32[3,32,512]{2,1,0:T(8,128)S(1)} %pad_maximum_fusion.1), channel_id=1, source_target_pairs={{0,4},{4,8},{8,12},{12,16},{16,20},{20,24},{24,28},{1,5},{5,9},{9,... | collective-permute-start | bytes 589832 | tf_op jit(solution)/shard_map/ppermute | solution.py:14
  10.4 0.9 and_reduce_fusion
  13.6 6.3 %all-to-all-start = ((bf16[8,32,512]{2,1,0:T(8,128)(2,1)}), bf16[8,32,512]{2,1,0:T(8,128)(2,1)S(1)}, u32[]{:S(2)}, u32[]{:S(2)}) async-start(bf16[8,32,512]{2,1,0:T(8,128)(2,1)} %broadcast_select_fusion), calls=%async_computation | async-start | bytes 524288 | tf_op jit(solution)/shard_map/all_to_all | solution.py:80
  19.9 1.1 slice.146
  21.0 1.1 slice.145
  22.3 4.6 %collective-permute-start.3 = (f32[32,3,512]{2,1,0:T(4,128)S(1)}, f32[32,3,512]{2,1,0:T(4,128)S(1)}, u32[]{:S(2)}, u32[]{:S(2)}) collective-permute-start(f32[32,3,512]{2,1,0:T(4,128)S(1)} %pad_maximum_fusion), channel_id=1, source_target_pairs={{0,1},{1,2},{2,3},{4,5},{5,6},{6,7},{8,9},{9,10},{10,11},{12,13},{... | collective-permute-start | bytes 589832 | tf_op jit(solution)/shard_map/ppermute | solution.py:14
  26.9 1.7 reduce-window.16
  29.1 67.1 %all-gather = s32[32,1,768]{2,1,0:T(1,128)S(1)} all-gather(s32[1,1,768]{2,1,0:T(1,128)S(1)} %reshape.220), channel_id=1, replica_groups=mesh['gx'=8,'gy'=4] {'gx','gy'}, dimensions={0}, use_global_device_ids=true | all-gather | bytes 101376 | tf_op jit(solution)/shard_map/all_gather | solution.py:45
  96.5 1.7 reduce-window.14
  99.1 4.0 %fusion.4 = bf16[1536,1024]{1,0:T(8,128)(2,1)} fusion(bf16[768,1024]{1,0:T(8,128)(2,1)S(1)} %bitcast.129, s32[768]{0:T(1024)S(1)} %get-tuple-element.55), kind=kOutput, calls=%fused_computation.8 | convolution fusion | flops 2418671616 | bytes 4721664 | tf_op jit(solution)/shard_map/dot_general | solution.py:39
  104.1 3.9 %all-to-all-start.1 = ((bf16[32,48,1024]{2,1,0:T(8,128)(2,1)}), bf16[32,48,1024]{2,1,0:T(8,128)(2,1)}, u32[]{:S(2)}, u32[]{:S(2)}) async-start(bf16[32,48,1024]{2,1,0:T(8,128)(2,1)} %bitcast.126), calls=%async_computation.1 | async-start | bytes 6291456 | tf_op jit(solution)/shard_map/all_to_all | solution.py:55
  108.0 1.5 slice.148
  109.6 1.7 slice.153
  111.3 1.9 slice.158
  113.3 7.7 %multiply_subtract_fusion.1 = (f32[32,32,512]{2,1,0:T(8,128)}, f32[32,32,512]{2,1,0:T(8,128)}, f32[32,32,512]{2,1,0:T(8,128)S(1)}) fusion(f32[32,32,512]{2,1,0:T(8,128)} %param.15, f32[32,32,512]{2,1,0:T(8,128)S(1)} %copy-done.2, f32[32,32,511]{2,1,0:T(8,128)} %slice.158, f32[32,32,512]{2,1,0:T(8,128)} %param.16, f32[32,32,512]{2,1,0:T(8,128)} %param.14, ...), kind=kLoop, calls=%fused_computation.41 | loop fusion | flops 8388608 | bytes 23064576 | tf_op jit(solution)/shard_map/sub | solution.py:117
  121.0 1.6 slice.176
  123.2 55.8 %all-to-all-done.1 = bf16[32,48,1024]{2,1,0:T(8,128)(2,1)} async-done(((bf16[32,48,1024]{2,1,0:T(8,128)(2,1)}), bf16[32,48,1024]{2,1,0:T(8,128)(2,1)}, u32[]{:S(2)}, u32[]{:S(2)}) %all-to-all-start.1) | async-done | bytes 3145760 | tf_op jit(solution)/shard_map/all_to_all | solution.py:55
  179.0 4.7 %copy.38 = bf16[1536,1024]{0,1:T(8,128)(2,1)} copy(bf16[1536,1024]{1,0:T(8,128)(2,1)} %bitcast.4) | data formatting | bytes 6291456 | tf_op jit(solution)/shard_map/reshape | solution.py:66
  183.7 5.5 %fusion = f32[32,32,2,512]{3,1,2,0:T(8,128)S(1)} fusion(bf16[2,512,1536,1]{2,1,0,3:T(8,128)(2,1)} %bitcast.127, s32[1536]{0:T(1024)S(1)} %eq.113, s32[32,32]{1,0:T(8,128)S(1)} %multiply_add_fusion), kind=kOutput, calls=%fused_computation.1 | convolution fusion | flops 3222798336 | bytes 7350272 | tf_op jit(solution)/shard_map/dot_general | solution.py:65
  189.7 1.1 copy-done.3
  192.6 2.5 %fusion.14 = f32[32,32,512]{2,1,0:T(8,128)S(1)} fusion(f32[32,32,512]{2,1,0:T(8,128)S(1)} %copy-done.2, f32[32,32,512]{2,1,0:T(8,128)S(1)} %get-tuple-element.36, f32[32,32,512]{2,1,0:T(8,128)S(1)} %copy-done.7, f32[31,32,512]{2,1,0:T(8,128)S(1)} %copy-done.11, f32[1,32,512]{2,1,0:T(8,128)S(1)} %get-tuple-element.33, f32[32,32,512]{2,1,0:T(8,128)S(1)} %copy-done.5, ...), kind=kLoop, calls=%fused_computation.22 | loop fusion | flops 7864320 | bytes 20967424 | tf_op jit(solution)/shard_map/add | solution.py:126
  195.2 1.5 collective-permute-start.5
  196.8 3.4 %collective-permute-start.7 = (f32[32,1,512]{2,1,0:T(1,128)S(1)}, f32[32,1,512]{2,1,0:T(1,128)S(1)}, u32[]{:S(2)}, u32[]{:S(2)}) collective-permute-start(f32[32,1,512]{2,1,0:T(1,128)S(1)} %slice.186), channel_id=1, source_target_pairs={{0,1},{1,2},{2,3},{4,5},{5,6},{6,7},{8,9},{9,10},{10,11},{12,13},{... | collective-permute-start | bytes 196616 | tf_op jit(solution)/shard_map/ppermute | solution.py:14
  200.3 1.3 collective-permute-start.4
  202.3 1.3 collective-permute-start.6
  204.8 4.0 %collective-permute-done.6 = f32[32,1,512]{2,1,0:T(1,128)S(1)} collective-permute-done((f32[32,1,512]{2,1,0:T(1,128)S(1)}, f32[32,1,512]{2,1,0:T(1,128)S(1)}, u32[]{:S(2)}, u32[]{:S(2)}) %collective-permute-start.6) | collective-permute-done | bytes 65568 | tf_op jit(solution)/shard_map/ppermute | solution.py:14
  208.8 2.8 %multiply_subtract_fusion = (f32[32,32,512]{2,1,0:T(8,128)S(1)}, f32[32,32,512]{2,1,0:T(8,128)S(1)}, f32[32,32,512]{2,1,0:T(8,128)S(1)}) fusion(f32[32,32,512]{2,1,0:T(8,128)S(1)} %copy-done.4, f32[32,32,512]{2,1,0:T(8,128)S(1)} %fusion.14, f32[32,32,511]{2,1,0:T(8,128)S(1)} %slice.188, f32[32,32,512]{2,1,0:T(8,128)S(1)} %copy-done.3, ...), kind=kLoop, calls=%fused_computation.40 | loop fusion | flops 8388608 | bytes 23064576 | tf_op jit(solution)/shard_map/sub | solution.py:117
  211.9 3.6 %fusion.23 = f32[32,32,512]{2,1,0:T(8,128)} fusion(f32[32,32,512]{2,1,0:T(8,128)S(1)} %fusion.14, f32[32,32,512]{2,1,0:T(8,128)S(1)} %get-tuple-element.35, f32[32,32,512]{2,1,0:T(8,128)S(1)} %get-tuple-element.39, f32[31,32,512]{2,1,0:T(8,128)S(1)} %slice.183, f32[1,32,512]{2,1,0:T(8,128)S(1)} %get-tuple-element.47, ...), kind=kLoop, calls=%fused_computation.35 | loop fusion | flops 7864320 | bytes 20967424 | tf_op jit(solution)/shard_map/add | solution.py:126
  (76 shorter events, 12.0 us)
Async XLA Ops:
  0.6 11.6 %copy-start = (bf16[16,32,512]{2,1,0:T(8,128)(2,1)S(1)}, bf16[16,32,512]{2,1,0:T(8,128)(2,1)}, u32[]{:S(2)}) copy-start(bf16[16,32,512]{2,1,0:T(8,128)(2,1)} %param.20) | copy-start | bytes 1572868
  0.6 26.2 %copy-start.14 = (s32[768,1]{0,1:T(1,128)S(1)}, s32[768,1]{0,1:T(1,128)}, u32[]{:S(2)}) copy-start(s32[768,1]{0,1:T(1,128)} %param.18) | copy-start | bytes 9220
  0.7 28.4 %copy-start.13 = (s32[768]{0:T(1024)S(1)}, s32[768]{0:T(1024)}, u32[]{:S(2)}) copy-start(s32[768]{0:T(1024)} %param.19) | copy-start | bytes 9220
  2.0 102.0 %collective-permute-start.1 = (f32[32,1,512]{2,1,0:T(1,128)S(1)}, f32[32,1,512]{2,1,0:T(1,128)S(1)}, u32[]{:S(2)}, u32[]{:S(2)}) collective-permute-start(f32[32,1,512]{2,1,0:T(1,128)S(1)} %get-tuple-element.50), channel_id=1, source_target_pairs={{1,0},{2,1},{3,2},{5,4},{6,5},{7,6},{9,8},{10,9},{11,10},{13,12},{... | collective-permute-start | bytes 196616 | tf_op jit(solution)/shard_map/ppermute | solution.py:14
  4.2 99.9 %collective-permute-start = (f32[1,32,512]{2,1,0:T(8,128)S(1)}, f32[1,32,512]{2,1,0:T(8,128)S(1)}, u32[]{:S(2)}, u32[]{:S(2)}) collective-permute-start(f32[1,32,512]{2,1,0:T(8,128)S(1)} %get-tuple-element.52), channel_id=1, source_target_pairs={{4,0},{8,4},{12,8},{16,12},{20,16},{24,20},{28,24},{5,1},{9,5},{13... | collective-permute-start | bytes 196616 | tf_op jit(solution)/shard_map/ppermute | solution.py:14
  7.2 91.5 %copy-start.12 = (bf16[768,2,512]{2,1,0:T(2,128)(2,1)S(1)}, bf16[768,2,512]{2,1,0:T(2,128)(2,1)}, u32[]{:S(2)}) copy-start(bf16[768,2,512]{2,1,0:T(2,128)(2,1)} %param.17) | copy-start | bytes 4718596
  7.3 96.9 %collective-permute-start.2 = (f32[3,32,512]{2,1,0:T(8,128)S(1)}, f32[3,32,512]{2,1,0:T(8,128)S(1)}, u32[]{:S(2)}, u32[]{:S(2)}) collective-permute-start(f32[3,32,512]{2,1,0:T(8,128)S(1)} %pad_maximum_fusion.1), channel_id=1, source_target_pairs={{0,4},{4,8},{8,12},{12,16},{16,20},{20,24},{24,28},{1,5},{5,9},{9,... | collective-permute-start | bytes 589832 | tf_op jit(solution)/shard_map/ppermute | solution.py:14
  13.6 90.4 %all-to-all-start = ((bf16[8,32,512]{2,1,0:T(8,128)(2,1)}), bf16[8,32,512]{2,1,0:T(8,128)(2,1)S(1)}, u32[]{:S(2)}, u32[]{:S(2)}) async-start(bf16[8,32,512]{2,1,0:T(8,128)(2,1)} %broadcast_select_fusion), calls=%async_computation | async-start | bytes 524288 | tf_op jit(solution)/shard_map/all_to_all | solution.py:80
  22.3 81.8 %collective-permute-start.3 = (f32[32,3,512]{2,1,0:T(4,128)S(1)}, f32[32,3,512]{2,1,0:T(4,128)S(1)}, u32[]{:S(2)}, u32[]{:S(2)}) collective-permute-start(f32[32,3,512]{2,1,0:T(4,128)S(1)} %pad_maximum_fusion), channel_id=1, source_target_pairs={{0,1},{1,2},{2,3},{4,5},{5,6},{6,7},{8,9},{9,10},{10,11},{12,13},{... | collective-permute-start | bytes 589832 | tf_op jit(solution)/shard_map/ppermute | solution.py:14
  104.1 3.9 %copy-start.2 = (f32[32,32,512]{2,1,0:T(8,128)S(1)}, f32[32,32,512]{2,1,0:T(8,128)}, u32[]{:S(2)}) copy-start(f32[32,32,512]{2,1,0:T(8,128)} %param.12) | copy-start | bytes 6291460
  104.1 74.8 %all-to-all-start.1 = ((bf16[32,48,1024]{2,1,0:T(8,128)(2,1)}), bf16[32,48,1024]{2,1,0:T(8,128)(2,1)}, u32[]{:S(2)}, u32[]{:S(2)}) async-start(bf16[32,48,1024]{2,1,0:T(8,128)(2,1)} %bitcast.126), calls=%async_computation.1 | async-start | bytes 6291456 | tf_op jit(solution)/shard_map/all_to_all | solution.py:55
  121.0 2.0 copy-start.6
  183.7 6.0 %copy-start.11 = (f32[31,32,512]{2,1,0:T(8,128)S(1)}, f32[31,32,512]{2,1,0:T(8,128)}, u32[]{:S(2)}) copy-start(f32[31,32,512]{2,1,0:T(8,128)} %slice.176) | copy-start | bytes 6094852
  189.2 1.6 copy-start.3
  189.2 2.2 %copy-start.4 = (f32[32,32,512]{2,1,0:T(8,128)S(1)}, f32[32,32,512]{2,1,0:T(8,128)}, u32[]{:S(2)}) copy-start(f32[32,32,512]{2,1,0:T(8,128)} %get-tuple-element.42) | copy-start | bytes 6291460
  189.2 2.8 %copy-start.5 = (f32[32,32,512]{2,1,0:T(8,128)S(1)}, f32[32,32,512]{2,1,0:T(8,128)}, u32[]{:S(2)}) copy-start(f32[32,32,512]{2,1,0:T(8,128)} %get-tuple-element.43) | copy-start | bytes 6291460
  189.2 3.4 %copy-start.7 = (f32[32,32,512]{2,1,0:T(8,128)S(1)}, f32[32,32,512]{2,1,0:T(8,128)}, u32[]{:S(2)}) copy-start(f32[32,32,512]{2,1,0:T(8,128)} %copy-done.6) | copy-start | bytes 6291460
  195.2 5.1 %collective-permute-start.5 = (f32[1,32,512]{2,1,0:T(8,128)S(1)}, f32[1,32,512]{2,1,0:T(8,128)S(1)}, u32[]{:S(2)}, u32[]{:S(2)}) collective-permute-start(f32[1,32,512]{2,1,0:T(8,128)S(1)} %slice.182), channel_id=1, source_target_pairs={{0,4},{4,8},{8,12},{12,16},{16,20},{20,24},{24,28},{1,5},{5,9},{9,... | collective-permute-start | bytes 196616 | tf_op jit(solution)/shard_map/ppermute | solution.py:14
  196.8 5.3 %collective-permute-start.7 = (f32[32,1,512]{2,1,0:T(1,128)S(1)}, f32[32,1,512]{2,1,0:T(1,128)S(1)}, u32[]{:S(2)}, u32[]{:S(2)}) collective-permute-start(f32[32,1,512]{2,1,0:T(1,128)S(1)} %slice.186), channel_id=1, source_target_pairs={{0,1},{1,2},{2,3},{4,5},{5,6},{6,7},{8,9},{9,10},{10,11},{12,13},{... | collective-permute-start | bytes 196616 | tf_op jit(solution)/shard_map/ppermute | solution.py:14
  200.3 4.5 %collective-permute-start.4 = (f32[1,32,512]{2,1,0:T(8,128)S(1)}, f32[1,32,512]{2,1,0:T(8,128)S(1)}, u32[]{:S(2)}, u32[]{:S(2)}) collective-permute-start(f32[1,32,512]{2,1,0:T(8,128)S(1)} %get-tuple-element.48), channel_id=1, source_target_pairs={{4,0},{8,4},{12,8},{16,12},{20,16},{24,20},{28,24},{5,1},{9,5},{13... | collective-permute-start | bytes 196616 | tf_op jit(solution)/shard_map/ppermute | solution.py:14
  202.3 6.5 %collective-permute-start.6 = (f32[32,1,512]{2,1,0:T(1,128)S(1)}, f32[32,1,512]{2,1,0:T(1,128)S(1)}, u32[]{:S(2)}, u32[]{:S(2)}) collective-permute-start(f32[32,1,512]{2,1,0:T(1,128)S(1)} %get-tuple-element.46), channel_id=1, source_target_pairs={{1,0},{2,1},{3,2},{5,4},{6,5},{7,6},{9,8},{10,9},{11,10},{13,12},{... | collective-permute-start | bytes 196616 | tf_op jit(solution)/shard_map/ppermute | solution.py:14
  211.6 4.0 %copy-start.8 = (f32[32,32,512]{2,1,0:T(8,128)}, f32[32,32,512]{2,1,0:T(8,128)S(1)}, u32[]{:S(2)}) copy-start(f32[32,32,512]{2,1,0:T(8,128)S(1)} %get-tuple-element.37) | copy-start | bytes 6291460
  211.6 4.0 %copy-start.9 = (f32[32,32,512]{2,1,0:T(8,128)}, f32[32,32,512]{2,1,0:T(8,128)S(1)}, u32[]{:S(2)}) copy-start(f32[32,32,512]{2,1,0:T(8,128)S(1)} %get-tuple-element.38) | copy-start | bytes 6291460
  211.6 3.9 %copy-start.10 = (f32[32,32,512]{2,1,0:T(8,128)}, f32[32,32,512]{2,1,0:T(8,128)S(1)}, u32[]{:S(2)}) copy-start(f32[32,32,512]{2,1,0:T(8,128)S(1)} %get-tuple-element.39) | copy-start | bytes 6291460
  211.9 3.7 %copy-start.1 = (bf16[16,32,512]{2,1,0:T(8,128)(2,1)S(1)}, bf16[16,32,512]{2,1,0:T(8,128)(2,1)}, u32[]{:S(2)}) copy-start(bf16[16,32,512]{2,1,0:T(8,128)(2,1)} %param.20) | copy-start | bytes 1572868
where the time goes:
time: 217 us; the launch traced here: 216 us
  blocking collectives  67.1 us (31%)
  waiting for transfers between devices  60.3 us (28%)
  starting transfers between devices  28.1 us (13%)
  other arithmetic  24.9 us (11%)
  local copies, waits for them, and re-layouts  24.5 us (11%)
  matrix products  9.48 us (4%)
    all_gather x1, blocking collectives, bubble_source(): lax.all_gather(code, ('gx', 'gy'), axis=0, tiled=True)  67.1 us
    all_to_all x1, waiting for transfers between devices, bubble_source(): lax.all_to_all(outgoing.reshape(devices, capacity, steps * depth), ('gx',...  55.8 us
    ppermute x8, starting transfers between devices, from_behind(): return lax.ppermute(block, axis, route)  17.9 us
    sub x2, other arithmetic, body(): vel_z = vel_z - step_ratio * buoyancy * (next_z - pressure)  10.5 us
    all_to_all x1, starting transfers between devices, incident_plane(): rows = lax.all_to_all(chosen, 'gx', split_axis=0, concat_axis=0, tiled=True)  6.32 us
    add x2, other arithmetic, body(): pressure + step_ratio * stiffness * (source[:, :, step, :] + forcing - di...  6.18 us
    dot_general x1, matrix products, bubble_source(): jnp.dot(hits, incoming.reshape(slots, steps * depth), preferred_element_t...  5.48 us
    reshape x1, local copies, waits for them, and re-layouts, bubble_source(): incoming.reshape(slots, steps * depth)  4.69 us
  transfers between devices with their start and end apart: 10, of which 3 were waited for; matrix products, arithmetic and copies ran while one was open for 16% of the time, Pallas kernels for 0%

commit v1 on v0

--- a/solution.py
+++ b/solution.py
@@ -6,6 +6,18 @@
 step_ratio = 0.4
 gas_density = 0.001
 gas_stiffness = 5.29e-05
+
+
+def collect(x, axis, dim):
+    ways, here = (lax.axis_size(axis), lax.axis_index(axis))
+    grown, reach = (x, 1)
+    while reach < ways:
+        theirs = lax.ppermute(grown, axis, [(d, d ^ reach) for d in range(ways)])
+        mine_first = jnp.concatenate([grown, theirs], axis=dim)
+        theirs_first = jnp.concatenate([theirs, grown], axis=dim)
+        grown = jnp.where(here & reach == 0, mine_first, theirs_first)
+        reach = 2 * reach
+    return grown
 
 
 def from_behind(block, axis, distance):
@@ -42,7 +54,7 @@
         preferred_element_type=jnp.float32,
     ).astype(jnp.bfloat16)
     code = dest * cells + bubble_column
-    all_code = lax.all_gather(code, ("gx", "gy"), axis=0, tiled=True).reshape(devices, bubbles)
+    all_code = collect(code, ("gx", "gy"), 0).reshape(devices, bubbles)
     all_dest = all_code // cells
     all_col = all_code % cells
     mine = (all_dest == me).astype(jnp.int32)

time: 217 us -> 168 us (0.77)
  blocking collectives: 67.1 us -> 0 us
  starting transfers between devices: 28.1 us -> 38.2 us
  waiting for transfers between devices: 60.3 us -> 67.3 us
    all_gather x1 -> x0, blocking collectives: 67.1 us -> none  [bubble_source(): lax.all_gather(code, ('gx', 'gy'), axis=0, tiled=True)]
    ppermute x0 -> x5, starting transfers between devices: none -> 9.66 us  [collect(): theirs = lax.ppermute(grown, axis, [(d, d ^ reach) for d in range(ways)])]
    ppermute x0 -> x5, waiting for transfers between devices: none -> 7 us  [collect(): theirs = lax.ppermute(grown, axis, [(d, d ^ reach) for d in range(ways)])]
  transfers between devices with their start and end apart: 10 -> 15, of which waited for: 3 -> 7; matrix products, arithmetic and copies ran while one was open for 16% -> 20% of each run, Pallas kernels for 0% -> 0%
where the time goes in v1:
time: 168 us; the launch traced here: 167 us
  waiting for transfers between devices  67.3 us (40%)
  starting transfers between devices  38.2 us (23%)
  other arithmetic  26.3 us (16%)
  local copies, waits for them, and re-layouts  24.5 us (15%)
  matrix products  9.47 us (6%)
    all_to_all x1, waiting for transfers between devices, bubble_source(): lax.all_to_all(outgoing.reshape(devices, capacity, steps * depth), ('gx',...  55.8 us
    ppermute x8, starting transfers between devices, from_behind(): return lax.ppermute(block, axis, route)  17.7 us
    sub x2, other arithmetic, body(): vel_z = vel_z - step_ratio * buoyancy * (next_z - pressure)  10.5 us
    ppermute x5, starting transfers between devices, collect(): theirs = lax.ppermute(grown, axis, [(d, d ^ reach) for d in range(ways)])  9.66 us
    ppermute x5, waiting for transfers between devices, collect(): theirs = lax.ppermute(grown, axis, [(d, d ^ reach) for d in range(ways)])  7 us
    add x2, other arithmetic, body(): pressure + step_ratio * stiffness * (source[:, :, step, :] + forcing - di...  6.18 us
    all_to_all x1, starting transfers between devices, bubble_source(): lax.all_to_all(outgoing.reshape(devices, capacity, steps * depth), ('gx',...  5.93 us
    dot_general x1, matrix products, bubble_source(): jnp.dot(hits, incoming.reshape(slots, steps * depth), preferred_element_t...  5.48 us
  transfers between devices with their start and end apart: 15, of which 7 were waited for; matrix products, arithmetic and copies ran while one was open for 20% of the time, Pallas kernels for 0%

profile of v1, /device:TPU:0, one launch (start us, length us, event | category | flops | bytes accessed | tf_op | source)
XLA Modules:
  0.0 167.2 jit_solution(10494521352324703895)
XLA Ops:
  1.5 1.7 %reduce-window.16 = s32[32,6,128]{2,0,1:T(8,128)S(1)} reduce-window(s32[32,6,128]{2,0,1:T(8,128)S(1)} %fusion.34, s32[]{:T(128)} %constant.126.clone.1), window={size=1x1x128 pad=0_0x0_0x127_0}, to_apply=%region_3.4 | reduce-window | flops 3121152 | bytes 196612 | tf_op jit(solution)/shard_map/reduce-window.2
  4.4 2.9 %collective-permute-start = (s32[768]{0:T(1024)S(1)}, s32[768]{0:T(1024)S(1)}, u32[]{:S(2)}, u32[]{:S(2)}) collective-permute-start(s32[768]{0:T(1024)S(1)} %get-tuple-element.56), channel_id=1, source_target_pairs={{0,1},{1,0},{2,3},{3,2},{4,5},{5,4},{6,7},{7,6},{8,9},{9,8},{10,11... | collective-permute-start | bytes 9224 | tf_op jit(solution)/shard_map/ppermute | solution.py:15
  7.3 1.3 fusion.48
  8.6 1.3 collective-permute-start.6
  10.8 1.3 collective-permute-start.5
  13.8 3.0 %collective-permute-start.7 = (f32[3,32,512]{2,1,0:T(8,128)S(1)}, f32[3,32,512]{2,1,0:T(8,128)S(1)}, u32[]{:S(2)}, u32[]{:S(2)}) collective-permute-start(f32[3,32,512]{2,1,0:T(8,128)S(1)} %pad_maximum_fusion.1), channel_id=1, source_target_pairs={{0,4},{4,8},{8,12},{12,16},{16,20},{20,24},{24,28},{1,5},{5,9},{9,... | collective-permute-start | bytes 589832 | tf_op jit(solution)/shard_map/ppermute | solution.py:26
  20.0 4.9 %all-to-all-start = ((bf16[8,32,512]{2,1,0:T(8,128)(2,1)}), bf16[8,32,512]{2,1,0:T(8,128)(2,1)S(1)}, u32[]{:S(2)}, u32[]{:S(2)}) async-start(bf16[8,32,512]{2,1,0:T(8,128)(2,1)} %broadcast_select_fusion), calls=%async_computation | async-start | bytes 524288 | tf_op jit(solution)/shard_map/all_to_all | solution.py:92
  27.3 4.6 %collective-permute-start.8 = (f32[32,3,512]{2,1,0:T(4,128)S(1)}, f32[32,3,512]{2,1,0:T(4,128)S(1)}, u32[]{:S(2)}, u32[]{:S(2)}) collective-permute-start(f32[32,3,512]{2,1,0:T(4,128)S(1)} %pad_maximum_fusion), channel_id=1, source_target_pairs={{0,1},{1,2},{2,3},{4,5},{5,6},{6,7},{8,9},{9,10},{10,11},{12,13},{... | collective-permute-start | bytes 589832 | tf_op jit(solution)/shard_map/ppermute | solution.py:26
  32.3 4.0 %fusion.4 = bf16[1536,1024]{1,0:T(8,128)(2,1)} fusion(bf16[768,1024]{1,0:T(8,128)(2,1)S(1)} %bitcast.80, s32[768]{0:T(1024)S(1)} %get-tuple-element.55), kind=kOutput, calls=%fused_computation.8 | convolution fusion | flops 2418671616 | bytes 4721664 | tf_op jit(solution)/shard_map/dot_general | solution.py:51
  36.3 1.6 collective-permute-start.1
  37.9 2.1 %collective-permute-done.1 = s32[1536]{0:T(1024)S(1)} collective-permute-done((s32[1536]{0:T(1024)S(1)}, s32[1536]{0:T(1024)S(1)}, u32[]{:S(2)}, u32[]{:S(2)}) %collective-permute-start.1) | collective-permute-done | bytes 6176 | tf_op jit(solution)/shard_map/ppermute | solution.py:15
  41.3 2.1 %collective-permute-start.3 = (s32[6144]{0:T(1024)S(1)}, s32[6144]{0:T(1024)S(1)}, u32[]{:S(2)}, u32[]{:S(2)}) collective-permute-start(s32[6144]{0:T(1024)S(1)} %add_select_fusion.9), channel_id=1, source_target_pairs={{0,8},{1,9},{2,10},{3,11},{4,12},{5,13},{6,14},{7,15},{8,0},{9,1},... | collective-permute-start | bytes 73736 | tf_op jit(solution)/shard_map/ppermute | solution.py:15
  43.4 1.8 %collective-permute-done.3 = s32[6144]{0:T(1024)S(1)} collective-permute-done((s32[6144]{0:T(1024)S(1)}, s32[6144]{0:T(1024)S(1)}, u32[]{:S(2)}, u32[]{:S(2)}) %collective-permute-start.3) | collective-permute-done | bytes 24608 | tf_op jit(solution)/shard_map/ppermute | solution.py:15
  45.2 3.0 %collective-permute-start.4 = (s32[12288]{0:T(1024)S(1)}, s32[12288]{0:T(1024)S(1)}, u32[]{:S(2)}, u32[]{:S(2)}) collective-permute-start(s32[12288]{0:T(1024)S(1)} %add_select_fusion.6), channel_id=1, source_target_pairs={{0,16},{1,17},{2,18},{3,19},{4,20},{5,21},{6,22},{7,23},{8,24},{9,... | collective-permute-start | bytes 147464 | tf_op jit(solution)/shard_map/ppermute | solution.py:15
  48.2 2.1 %collective-permute-done.4 = s32[12288]{0:T(1024)S(1)} collective-permute-done((s32[12288]{0:T(1024)S(1)}, s32[12288]{0:T(1024)S(1)}, u32[]{:S(2)}, u32[]{:S(2)}) %collective-permute-start.4) | collective-permute-done | bytes 49184 | tf_op jit(solution)/shard_map/ppermute | solution.py:15
  50.4 1.7 %reduce-window.14 = s32[32,6,128]{2,0,1:T(8,128)S(1)} reduce-window(s32[32,6,128]{2,0,1:T(8,128)S(1)} %fusion.35, s32[]{:T(128)} %constant.126.clone.1), window={size=1x1x128 pad=0_0x0_0x127_0}, to_apply=%region_0.1 | reduce-window | flops 3121152 | bytes 196612 | tf_op jit(solution)/shard_map/reduce-window
  53.6 5.9 %all-to-all-start.1 = ((bf16[32,48,1024]{2,1,0:T(8,128)(2,1)}), bf16[32,48,1024]{2,1,0:T(8,128)(2,1)}, u32[]{:S(2)}, u32[]{:S(2)}) async-start(bf16[32,48,1024]{2,1,0:T(8,128)(2,1)} %bitcast.77), calls=%async_computation.1 | async-start | bytes 6291456 | tf_op jit(solution)/shard_map/all_to_all | solution.py:67
  59.5 1.5 slice.148
  61.1 1.7 %slice.153 = f32[32,31,512]{2,1,0:T(8,128)} slice(f32[32,32,512]{2,1,0:T(8,128)S(1)} %copy-done.2), slice={[0:32], [1:32], [0:512]} | slice | bytes 4063232 | tf_op jit(solution)/shard_map/slice | solution.py:125
  62.8 1.9 %slice.158 = f32[32,32,511]{2,1,0:T(8,128)} slice(f32[32,32,512]{2,1,0:T(8,128)S(1)} %copy-done.2), slice={[0:32], [0:32], [1:512]} | slice | bytes 4186112 | tf_op jit(solution)/shard_map/slice | solution.py:126
  64.8 7.7 %multiply_subtract_fusion.1 = (f32[32,32,512]{2,1,0:T(8,128)}, f32[32,32,512]{2,1,0:T(8,128)}, f32[32,32,512]{2,1,0:T(8,128)S(1)}) fusion(f32[32,32,512]{2,1,0:T(8,128)} %param.15, f32[32,32,512]{2,1,0:T(8,128)S(1)} %copy-done.2, f32[32,32,511]{2,1,0:T(8,128)} %slice.158, f32[32,32,512]{2,1,0:T(8,128)} %param.16, f32[32,32,512]{2,1,0:T(8,128)} %param.14, ...), kind=kLoop, calls=%fused_computation.41 | loop fusion | flops 8388608 | bytes 23064576 | tf_op jit(solution)/shard_map/sub | solution.py:129
  72.5 1.6 slice.176
  74.7 55.8 %all-to-all-done.1 = bf16[32,48,1024]{2,1,0:T(8,128)(2,1)} async-done(((bf16[32,48,1024]{2,1,0:T(8,128)(2,1)}), bf16[32,48,1024]{2,1,0:T(8,128)(2,1)}, u32[]{:S(2)}, u32[]{:S(2)}) %all-to-all-start.1) | async-done | bytes 3145760 | tf_op jit(solution)/shard_map/all_to_all | solution.py:67
  130.5 4.6 %copy.42 = bf16[1536,1024]{0,1:T(8,128)(2,1)} copy(bf16[1536,1024]{1,0:T(8,128)(2,1)} %bitcast.4) | data formatting | bytes 6291456 | tf_op jit(solution)/shard_map/reshape | solution.py:78
  135.1 5.5 %fusion = f32[32,32,2,512]{3,1,2,0:T(8,128)S(1)} fusion(bf16[2,512,1536,1]{2,1,0,3:T(8,128)(2,1)} %bitcast.78, s32[1536]{0:T(1024)S(1)} %eq.133, s32[32,32]{1,0:T(8,128)S(1)} %multiply_add_fusion), kind=kOutput, calls=%fused_computation.1 | convolution fusion | flops 3222798336 | bytes 7350272 | tf_op jit(solution)/shard_map/dot_general | solution.py:77
  144.1 2.5 %fusion.14 = f32[32,32,512]{2,1,0:T(8,128)S(1)} fusion(f32[32,32,512]{2,1,0:T(8,128)S(1)} %copy-done.2, f32[32,32,512]{2,1,0:T(8,128)S(1)} %get-tuple-element.36, f32[32,32,512]{2,1,0:T(8,128)S(1)} %copy-done.7, f32[31,32,512]{2,1,0:T(8,128)S(1)} %copy-done.11, f32[1,32,512]{2,1,0:T(8,128)S(1)} %get-tuple-element.33, f32[32,32,512]{2,1,0:T(8,128)S(1)} %copy-done.5, ...), kind=kLoop, calls=%fused_computation.22 | loop fusion | flops 7864320 | bytes 20967424 | tf_op jit(solution)/shard_map/add | solution.py:138
  146.7 1.5 collective-permute-start.10
  148.3 3.4 %collective-permute-start.12 = (f32[32,1,512]{2,1,0:T(1,128)S(1)}, f32[32,1,512]{2,1,0:T(1,128)S(1)}, u32[]{:S(2)}, u32[]{:S(2)}) collective-permute-start(f32[32,1,512]{2,1,0:T(1,128)S(1)} %slice.186), channel_id=1, source_target_pairs={{0,1},{1,2},{2,3},{4,5},{5,6},{6,7},{8,9},{9,10},{10,11},{12,13},{... | collective-permute-start | bytes 196616 | tf_op jit(solution)/shard_map/ppermute | solution.py:26
  153.7 1.3 collective-permute-start.11
  156.3 4.0 %collective-permute-done.11 = f32[32,1,512]{2,1,0:T(1,128)S(1)} collective-permute-done((f32[32,1,512]{2,1,0:T(1,128)S(1)}, f32[32,1,512]{2,1,0:T(1,128)S(1)}, u32[]{:S(2)}, u32[]{:S(2)}) %collective-permute-start.11) | collective-permute-done | bytes 65568 | tf_op jit(solution)/shard_map/ppermute | solution.py:26
  160.3 2.8 %multiply_subtract_fusion = (f32[32,32,512]{2,1,0:T(8,128)S(1)}, f32[32,32,512]{2,1,0:T(8,128)S(1)}, f32[32,32,512]{2,1,0:T(8,128)S(1)}) fusion(f32[32,32,512]{2,1,0:T(8,128)S(1)} %copy-done.4, f32[32,32,512]{2,1,0:T(8,128)S(1)} %fusion.14, f32[32,32,511]{2,1,0:T(8,128)S(1)} %slice.188, f32[32,32,512]{2,1,0:T(8,128)S(1)} %copy-done.3, ...), kind=kLoop, calls=%fused_computation.40 | loop fusion | flops 8388608 | bytes 23064576 | tf_op jit(solution)/shard_map/sub | solution.py:129
  163.4 3.6 %fusion.23 = f32[32,32,512]{2,1,0:T(8,128)} fusion(f32[32,32,512]{2,1,0:T(8,128)S(1)} %fusion.14, f32[32,32,512]{2,1,0:T(8,128)S(1)} %get-tuple-element.35, f32[32,32,512]{2,1,0:T(8,128)S(1)} %get-tuple-element.39, f32[31,32,512]{2,1,0:T(8,128)S(1)} %slice.183, f32[1,32,512]{2,1,0:T(8,128)S(1)} %get-tuple-element.47, ...), kind=kLoop, calls=%fused_computation.35 | loop fusion | flops 7864320 | bytes 20967424 | tf_op jit(solution)/shard_map/add | solution.py:138
  (104 shorter events, 21.0 us)
Async XLA Ops:
  0.6 18.0 %copy-start = (bf16[16,32,512]{2,1,0:T(8,128)(2,1)S(1)}, bf16[16,32,512]{2,1,0:T(8,128)(2,1)}, u32[]{:S(2)}) copy-start(bf16[16,32,512]{2,1,0:T(8,128)(2,1)} %param.20) | copy-start | bytes 1572868
  0.6 31.2 %copy-start.12 = (bf16[768,2,512]{2,1,0:T(2,128)(2,1)S(1)}, bf16[768,2,512]{2,1,0:T(2,128)(2,1)}, u32[]{:S(2)}) copy-start(bf16[768,2,512]{2,1,0:T(2,128)(2,1)} %param.17) | copy-start | bytes 4718596
  4.4 31.9 %collective-permute-start = (s32[768]{0:T(1024)S(1)}, s32[768]{0:T(1024)S(1)}, u32[]{:S(2)}, u32[]{:S(2)}) collective-permute-start(s32[768]{0:T(1024)S(1)} %get-tuple-element.56), channel_id=1, source_target_pairs={{0,1},{1,0},{2,3},{3,2},{4,5},{5,4},{6,7},{7,6},{8,9},{9,8},{10,11... | collective-permute-start | bytes 9224 | tf_op jit(solution)/shard_map/ppermute | solution.py:15
  8.6 44.9 %collective-permute-start.6 = (f32[32,1,512]{2,1,0:T(1,128)S(1)}, f32[32,1,512]{2,1,0:T(1,128)S(1)}, u32[]{:S(2)}, u32[]{:S(2)}) collective-permute-start(f32[32,1,512]{2,1,0:T(1,128)S(1)} %get-tuple-element.50), channel_id=1, source_target_pairs={{1,0},{2,1},{3,2},{5,4},{6,5},{7,6},{9,8},{10,9},{11,10},{13,12},{... | collective-permute-start | bytes 196616 | tf_op jit(solution)/shard_map/ppermute | solution.py:26
  10.8 42.7 %collective-permute-start.5 = (f32[1,32,512]{2,1,0:T(8,128)S(1)}, f32[1,32,512]{2,1,0:T(8,128)S(1)}, u32[]{:S(2)}, u32[]{:S(2)}) collective-permute-start(f32[1,32,512]{2,1,0:T(8,128)S(1)} %get-tuple-element.52), channel_id=1, source_target_pairs={{4,0},{8,4},{12,8},{16,12},{20,16},{24,20},{28,24},{5,1},{9,5},{13... | collective-permute-start | bytes 196616 | tf_op jit(solution)/shard_map/ppermute | solution.py:26
  13.8 39.7 %collective-permute-start.7 = (f32[3,32,512]{2,1,0:T(8,128)S(1)}, f32[3,32,512]{2,1,0:T(8,128)S(1)}, u32[]{:S(2)}, u32[]{:S(2)}) collective-permute-start(f32[3,32,512]{2,1,0:T(8,128)S(1)} %pad_maximum_fusion.1), channel_id=1, source_target_pairs={{0,4},{4,8},{8,12},{12,16},{16,20},{20,24},{24,28},{1,5},{5,9},{9,... | collective-permute-start | bytes 589832 | tf_op jit(solution)/shard_map/ppermute | solution.py:26
  20.0 33.4 %all-to-all-start = ((bf16[8,32,512]{2,1,0:T(8,128)(2,1)}), bf16[8,32,512]{2,1,0:T(8,128)(2,1)S(1)}, u32[]{:S(2)}, u32[]{:S(2)}) async-start(bf16[8,32,512]{2,1,0:T(8,128)(2,1)} %broadcast_select_fusion), calls=%async_computation | async-start | bytes 524288 | tf_op jit(solution)/shard_map/all_to_all | solution.py:92
  27.3 26.3 %collective-permute-start.8 = (f32[32,3,512]{2,1,0:T(4,128)S(1)}, f32[32,3,512]{2,1,0:T(4,128)S(1)}, u32[]{:S(2)}, u32[]{:S(2)}) collective-permute-start(f32[32,3,512]{2,1,0:T(4,128)S(1)} %pad_maximum_fusion), channel_id=1, source_target_pairs={{0,1},{1,2},{2,3},{4,5},{5,6},{6,7},{8,9},{9,10},{10,11},{12,13},{... | collective-permute-start | bytes 589832 | tf_op jit(solution)/shard_map/ppermute | solution.py:26
  36.3 3.7 %collective-permute-start.1 = (s32[1536]{0:T(1024)S(1)}, s32[1536]{0:T(1024)S(1)}, u32[]{:S(2)}, u32[]{:S(2)}) collective-permute-start(s32[1536]{0:T(1024)S(1)} %add_select_fusion.14), channel_id=1, source_target_pairs={{0,2},{1,3},{2,0},{3,1},{4,6},{5,7},{6,4},{7,5},{8,10},{9,11},{10,... | collective-permute-start | bytes 18440 | tf_op jit(solution)/shard_map/ppermute | solution.py:15
  40.0 1.2 collective-permute-start.2
  41.3 3.9 %collective-permute-start.3 = (s32[6144]{0:T(1024)S(1)}, s32[6144]{0:T(1024)S(1)}, u32[]{:S(2)}, u32[]{:S(2)}) collective-permute-start(s32[6144]{0:T(1024)S(1)} %add_select_fusion.9), channel_id=1, source_target_pairs={{0,8},{1,9},{2,10},{3,11},{4,12},{5,13},{6,14},{7,15},{8,0},{9,1},... | collective-permute-start | bytes 73736 | tf_op jit(solution)/shard_map/ppermute | solution.py:15
  45.2 5.1 %collective-permute-start.4 = (s32[12288]{0:T(1024)S(1)}, s32[12288]{0:T(1024)S(1)}, u32[]{:S(2)}, u32[]{:S(2)}) collective-permute-start(s32[12288]{0:T(1024)S(1)} %add_select_fusion.6), channel_id=1, source_target_pairs={{0,16},{1,17},{2,18},{3,19},{4,20},{5,21},{6,22},{7,23},{8,24},{9,... | collective-permute-start | bytes 147464 | tf_op jit(solution)/shard_map/ppermute | solution.py:15
  53.6 6.0 %copy-start.2 = (f32[32,32,512]{2,1,0:T(8,128)S(1)}, f32[32,32,512]{2,1,0:T(8,128)}, u32[]{:S(2)}) copy-start(f32[32,32,512]{2,1,0:T(8,128)} %param.12) | copy-start | bytes 6291460
  53.6 76.9 %all-to-all-start.1 = ((bf16[32,48,1024]{2,1,0:T(8,128)(2,1)}), bf16[32,48,1024]{2,1,0:T(8,128)(2,1)}, u32[]{:S(2)}, u32[]{:S(2)}) async-start(bf16[32,48,1024]{2,1,0:T(8,128)(2,1)} %bitcast.77), calls=%async_computation.1 | async-start | bytes 6291456 | tf_op jit(solution)/shard_map/all_to_all | solution.py:67
  72.5 2.0 %copy-start.6 = (f32[32,32,512]{2,1,0:T(8,128)}, f32[32,32,512]{2,1,0:T(8,128)S(1)}, u32[]{:S(2)}) copy-start(f32[32,32,512]{2,1,0:T(8,128)S(1)} %get-tuple-element.44) | copy-start | bytes 6291460
  135.1 6.0 %copy-start.11 = (f32[31,32,512]{2,1,0:T(8,128)S(1)}, f32[31,32,512]{2,1,0:T(8,128)}, u32[]{:S(2)}) copy-start(f32[31,32,512]{2,1,0:T(8,128)} %slice.176) | copy-start | bytes 6094852
  140.6 1.6 copy-start.3
  140.6 2.2 %copy-start.4 = (f32[32,32,512]{2,1,0:T(8,128)S(1)}, f32[32,32,512]{2,1,0:T(8,128)}, u32[]{:S(2)}) copy-start(f32[32,32,512]{2,1,0:T(8,128)} %get-tuple-element.42) | copy-start | bytes 6291460
  140.7 2.8 %copy-start.5 = (f32[32,32,512]{2,1,0:T(8,128)S(1)}, f32[32,32,512]{2,1,0:T(8,128)}, u32[]{:S(2)}) copy-start(f32[32,32,512]{2,1,0:T(8,128)} %get-tuple-element.43) | copy-start | bytes 6291460
  140.7 3.4 %copy-start.7 = (f32[32,32,512]{2,1,0:T(8,128)S(1)}, f32[32,32,512]{2,1,0:T(8,128)}, u32[]{:S(2)}) copy-start(f32[32,32,512]{2,1,0:T(8,128)} %copy-done.6) | copy-start | bytes 6291460
  146.7 5.0 %collective-permute-start.10 = (f32[1,32,512]{2,1,0:T(8,128)S(1)}, f32[1,32,512]{2,1,0:T(8,128)S(1)}, u32[]{:S(2)}, u32[]{:S(2)}) collective-permute-start(f32[1,32,512]{2,1,0:T(8,128)S(1)} %slice.182), channel_id=1, source_target_pairs={{0,4},{4,8},{8,12},{12,16},{16,20},{20,24},{24,28},{1,5},{5,9},{9,... | collective-permute-start | bytes 196616 | tf_op jit(solution)/shard_map/ppermute | solution.py:26
  148.3 5.3 %collective-permute-start.12 = (f32[32,1,512]{2,1,0:T(1,128)S(1)}, f32[32,1,512]{2,1,0:T(1,128)S(1)}, u32[]{:S(2)}, u32[]{:S(2)}) collective-permute-start(f32[32,1,512]{2,1,0:T(1,128)S(1)} %slice.186), channel_id=1, source_target_pairs={{0,1},{1,2},{2,3},{4,5},{5,6},{6,7},{8,9},{9,10},{10,11},{12,13},{... | collective-permute-start | bytes 196616 | tf_op jit(solution)/shard_map/ppermute | solution.py:26
  151.8 4.5 %collective-permute-start.9 = (f32[1,32,512]{2,1,0:T(8,128)S(1)}, f32[1,32,512]{2,1,0:T(8,128)S(1)}, u32[]{:S(2)}, u32[]{:S(2)}) collective-permute-start(f32[1,32,512]{2,1,0:T(8,128)S(1)} %get-tuple-element.48), channel_id=1, source_target_pairs={{4,0},{8,4},{12,8},{16,12},{20,16},{24,20},{28,24},{5,1},{9,5},{13... | collective-permute-start | bytes 196616 | tf_op jit(solution)/shard_map/ppermute | solution.py:26
  153.7 6.5 %collective-permute-start.11 = (f32[32,1,512]{2,1,0:T(1,128)S(1)}, f32[32,1,512]{2,1,0:T(1,128)S(1)}, u32[]{:S(2)}, u32[]{:S(2)}) collective-permute-start(f32[32,1,512]{2,1,0:T(1,128)S(1)} %get-tuple-element.46), channel_id=1, source_target_pairs={{1,0},{2,1},{3,2},{5,4},{6,5},{7,6},{9,8},{10,9},{11,10},{13,12},{... | collective-permute-start | bytes 196616 | tf_op jit(solution)/shard_map/ppermute | solution.py:26
  163.1 4.0 %copy-start.8 = (f32[32,32,512]{2,1,0:T(8,128)}, f32[32,32,512]{2,1,0:T(8,128)S(1)}, u32[]{:S(2)}) copy-start(f32[32,32,512]{2,1,0:T(8,128)S(1)} %get-tuple-element.37) | copy-start | bytes 6291460
  163.1 4.0 %copy-start.9 = (f32[32,32,512]{2,1,0:T(8,128)}, f32[32,32,512]{2,1,0:T(8,128)S(1)}, u32[]{:S(2)}) copy-start(f32[32,32,512]{2,1,0:T(8,128)S(1)} %get-tuple-element.38) | copy-start | bytes 6291460
  163.1 3.9 %copy-start.10 = (f32[32,32,512]{2,1,0:T(8,128)}, f32[32,32,512]{2,1,0:T(8,128)S(1)}, u32[]{:S(2)}) copy-start(f32[32,32,512]{2,1,0:T(8,128)S(1)} %get-tuple-element.39) | copy-start | bytes 6291460
  163.4 3.7 %copy-start.1 = (bf16[16,32,512]{2,1,0:T(8,128)(2,1)S(1)}, bf16[16,32,512]{2,1,0:T(8,128)(2,1)}, u32[]{:S(2)}) copy-start(bf16[16,32,512]{2,1,0:T(8,128)(2,1)} %param.20) | copy-start | bytes 1572868
